TPU v7x, 256 devices: a whole 4x4x8 slice. The times are simulated.
256 devices in a mesh: seq: 32 (over y, x, core), resp: 8 (over z).
Axes of the slice: x: 4, y: 4, z: 8, core: 2. Of those that a mesh axis runs over, the one named last changes fastest.
Arguments:
- prompt_grad: bfloat16 [32768, 4096], P('seq', 'resp'), may hold values from -0.119628906 to 0.119628906
- prompt_keys: bfloat16 [32768, 128], P('seq'), may hold values from -6 to 6
- prompt_queries: bfloat16 [32768, 128], P('seq'), may hold values from -0.52734375 to 0.52734375
- prompt_decay: float32 [64, 32768], P('resp', 'seq'), may hold values from -2 to 0
- resp_grad: bfloat16 [32768, 4096], P('resp', 'seq'), may hold values from -0.119628906 to 0.119628906
- resp_keys: bfloat16 [32768, 128], P('resp'), may hold values from -6 to 6
- resp_queries: bfloat16 [32768, 128], P('resp'), may hold values from -0.52734375 to 0.52734375
- resp_decay: float32 [64, 32768], P('seq', 'resp'), may hold values from -2 to 0
- resp_segment: int32 [32768], P('resp'), may hold values from 0 to 8, as said below
Outputs:
- prompt_dx: bfloat16 [32768, 4096], P('seq', 'resp')
- resp_dx: bfloat16 [32768, 4096], P('resp', 'seq')
Inputs may be any that keep to these rules, and one draw needn't show every extreme that they name: `resp_segment`: each aligned block of 4096 slots holds responses 0 to 7 in this order, each of one slot or more, then padding slots marked 8; a block holds 1024 live slots or more, and some block has no padding.
All inputs are finite; a program needn't handle non-finite values.
Results may differ from a plain program's by a relative error of at most 0.0057.
Values sent between devices are 32-bit elements; how exact they have to be, the bound alone decides.
No kernel may reach another device: no remote copies, remote signals or barrier semaphores. Data moves between devices by JAX's collectives and lax.ppermute only.
A program may use at most 64 MiB of HBM per device.

v0:
```python
import jax
import jax.numpy as jnp
from jax import lax
from jax.sharding import PartitionSpec as P

P_SIZE = 64
N = 128
GROUP = 256
RESP_DEV = 8


def group_parts(out_grad, queries, decay, segment, alive_mask):
    tokens = out_grad.shape[0]
    head_count = decay.shape[0]
    groups = tokens // GROUP
    cum_sums = jnp.cumsum(decay, axis=1)
    cum_group = cum_sums.reshape(head_count, groups, GROUP).transpose(1, 0, 2)
    decay_group = decay.reshape(head_count, groups, GROUP).transpose(1, 0, 2)
    before = cum_group[:, :, 0] - decay_group[:, :, 0]
    seg_group = segment.reshape(groups, GROUP)
    alive_group = alive_mask.reshape(groups, GROUP)
    first_label = seg_group[:, 0]
    last_label = seg_group[:, -1]
    grad_group = out_grad.reshape(groups, GROUP, head_count, P_SIZE)
    query_group = queries.reshape(groups, GROUP, N)
    keep_mask = (seg_group == first_label[:, None]) & alive_group
    factor = jnp.where(keep_mask[:, None, :], jnp.exp(cum_group - before[:, :, None]), 0.0)
    weighted = (factor.transpose(0, 2, 1)[:, :, :, None] * grad_group).astype(jnp.bfloat16)
    states = jnp.einsum("clhp,cln->chpn", weighted, query_group, preferred_element_type=jnp.float32)
    group_gains = jnp.exp(cum_group[:, :, -1] - before)
    joined = (first_label == last_label).astype(jnp.float32)
    linked = jnp.concatenate(
        [jnp.ones((1,), jnp.float32), (last_label[:-1] == first_label[1:]).astype(jnp.float32)]
    )
    flow = (
        joined[:, None]
        * group_gains
        * jnp.concatenate([linked[1:], jnp.zeros((1,), jnp.float32)])[:, None]
    )
    carry_at = jnp.arange(groups + 1)[:, None, None]
    state_at = jnp.arange(groups)[None, :, None]
    step_at = jnp.arange(groups)[None, None, :]
    inside = (carry_at <= step_at) & (step_at < state_at)
    spans = jnp.prod(jnp.where(inside[None], flow.T[:, None, None, :], 1.0), axis=3)
    link_at = jnp.concatenate([linked, jnp.zeros((1,), jnp.float32)])
    coef = (
        jnp.where((carry_at[:, :, 0] <= state_at[:, :, 0])[None], spans, 0.0)
        * link_at[None, :, None]
    )
    carries = jnp.einsum("hcd,dhpn->chpn", coef, states, precision=lax.Precision.HIGHEST)
    start_grad = carries[0]
    end_grads = carries[1:]
    return (
        cum_sums,
        cum_group,
        seg_group,
        alive_group,
        last_label,
        grad_group,
        end_grads,
        start_grad,
    )


def group_output(key_rows, queries, parts):
    cum_sums, cum_group, seg_group, alive_group, last_label, grad_group, end_grads, start_grad = (
        parts
    )
    groups = seg_group.shape[0]
    head_count = cum_group.shape[1]
    key_group = key_rows.reshape(groups, GROUP, N)
    query_group = queries.reshape(groups, GROUP, N)
    scores = jnp.einsum("csn,ctn->cst", query_group, key_group, preferred_element_type=jnp.float32)
    row_index = lax.broadcasted_iota(jnp.int32, (GROUP, GROUP), 0)
    col_index = lax.broadcasted_iota(jnp.int32, (GROUP, GROUP), 1)
    keep_mask = (
        (row_index >= col_index)[None]
        & (seg_group[:, :, None] == seg_group[:, None, :])
        & alive_group[:, :, None]
    )
    spread = cum_group[:, :, :, None] - cum_group[:, :, None, :]
    decays = jnp.exp(jnp.where(keep_mask[:, None], spread, -jnp.inf))
    mixing = (scores[:, None] * decays).astype(jnp.bfloat16)
    inner_part = jnp.einsum(
        "chst,cshp->cthp", mixing, grad_group, preferred_element_type=jnp.float32
    )
    across = jnp.einsum(
        "chpn,ctn->cthp",
        end_grads.astype(jnp.bfloat16),
        key_group,
        preferred_element_type=jnp.float32,
    )
    reach_weight = jnp.where(
        (seg_group == last_label[:, None])[:, None, :],
        jnp.exp(cum_group[:, :, -1:] - cum_group),
        0.0,
    )
    summed_parts = inner_part + across * reach_weight.transpose(0, 2, 1)[:, :, :, None]
    return summed_parts.reshape(groups * GROUP, head_count * P_SIZE)


def initial_state(out_grad, queries, decay, segment, alive_mask, cum_sums):
    tokens = out_grad.shape[0]
    head_count = decay.shape[0]
    firsts = jnp.concatenate([jnp.ones((1,), jnp.bool_), segment[1:] != segment[:-1]])
    labels = jnp.arange(RESP_DEV + 1, dtype=jnp.int32)
    member = segment[:, None] == labels[None, :]
    opening = cum_sums - decay
    base_label = jnp.sum(
        jnp.where((member & firsts[:, None])[None], opening[:, :, None], 0.0), axis=1
    )
    base_token = jnp.sum(jnp.where(member[None], base_label[:, None, :], 0.0), axis=2)
    factor = jnp.where(alive_mask[None], jnp.exp(cum_sums - base_token), 0.0)
    weighted = (factor.T[:, :, None] * out_grad.reshape(tokens, head_count, P_SIZE)).astype(
        jnp.bfloat16
    )
    return jnp.einsum("thp,tn->hpn", weighted, queries, preferred_element_type=jnp.float32)


def on_device(
    prompt_grad,
    prompt_keys,
    prompt_queries,
    prompt_decay,
    resp_grad,
    resp_keys,
    resp_queries,
    resp_decay,
    resp_segment,
):
    resp_alive = resp_segment < RESP_DEV
    resp_parts = group_parts(resp_grad, resp_queries, resp_decay, resp_segment, resp_alive)
    resp_dx = group_output(resp_keys, resp_queries, resp_parts).astype(jnp.bfloat16)
    partial_state = initial_state(
        resp_grad, resp_queries, resp_decay, resp_segment, resp_alive, resp_parts[0]
    )
    summed_state = lax.psum(partial_state, "resp")
    head_count = prompt_decay.shape[0]
    prompt_len = prompt_grad.shape[0]
    zero_label = jnp.zeros((prompt_len,), jnp.int32)
    all_alive = jnp.ones((prompt_len,), jnp.bool_)
    prompt_parts = group_parts(prompt_grad, prompt_queries, prompt_decay, zero_label, all_alive)
    cum_sums = prompt_parts[0]
    start_grad = prompt_parts[7]
    shard_total = cum_sums[:, -1]
    seq_index = lax.axis_index("seq")
    resp_index = lax.axis_index("resp")
    first_head = seq_index * summed_state.shape[0]
    owned = first_head // head_count == resp_index
    slots = lax.dynamic_update_slice_in_dim(
        jnp.zeros((head_count,) + summed_state.shape[1:], jnp.float32),
        summed_state,
        first_head % head_count,
        0,
    )
    my_heads = lax.psum(jnp.where(owned, slots, 0.0), "seq")
    span_len = lax.axis_size("seq")
    whole_b = start_grad
    whole_a = jnp.exp(shard_total)
    later_b = jnp.zeros_like(start_grad)
    later_a = jnp.ones_like(whole_a)
    shift = 1
    while shift < span_len:
        pairs = [(k + shift, k) for k in range(span_len - shift)]
        message = jnp.concatenate(
            [whole_b, jnp.broadcast_to(whole_a[:, None, None], (head_count, 1, N))], axis=1
        )
        got = lax.ppermute(message, "seq", pairs)
        valid = seq_index + shift < span_len
        got_b = jnp.where(valid, got[:, :P_SIZE], 0.0)
        got_a = jnp.where(valid, got[:, P_SIZE, 0], 1.0)
        later_b = later_b + later_a[:, None, None] * got_b
        later_a = later_a * got_a
        if shift * 2 < span_len:
            whole_b = whole_b + whole_a[:, None, None] * got_b
            whole_a = whole_a * got_a
        shift *= 2
    incoming = later_b + later_a[:, None, None] * my_heads
    local_part = group_output(prompt_keys, prompt_queries, prompt_parts)
    carry_term = jnp.einsum(
        "hpn,tn->thp",
        incoming.astype(jnp.bfloat16),
        prompt_keys,
        preferred_element_type=jnp.float32,
    )
    carry_term = carry_term * jnp.exp(shard_total[:, None] - cum_sums).T[:, :, None]
    prompt_dx = (local_part + carry_term.reshape(prompt_len, head_count * P_SIZE)).astype(
        jnp.bfloat16
    )
    return (prompt_dx, resp_dx)


def solution(mesh):
    return jax.shard_map(
        on_device,
        mesh=mesh,
        in_specs=(
            P("seq", "resp"),
            P("seq", None),
            P("seq", None),
            P("resp", "seq"),
            P("resp", "seq"),
            P("resp", None),
            P("resp", None),
            P("seq", "resp"),
            P("resp"),
        ),
        out_specs=(P("seq", "resp"), P("resp", "seq")),
        check_vma=False,
    )
```

profile of v0, /device:TPU:1, one launch (start us, length us, event | category | flops | bytes accessed | tf_op | source)
XLA Modules:
  0.0 240.0 jit_solution(917676850013422105)
XLA Ops:
  8.2 2.3 reduce-window.14
  17.5 3.8 %convolution_bitcast_fusion = f32[5,8,64,128]{3,0,2,1:T(8,128)} fusion(f32[8,5,4,1]{1,2,3,0:T(4,128)S(1)} %copy.138, f32[4,8,64,128]{3,2,1,0:T(8,128)S(1)} %fusion.28), kind=kOutput, calls=%fused_computation.29 | convolution fusion | flops 15728640 | bytes 2359936 | tf_op jit(solution)/shard_map/hcd,dhpn->chpn/dot_general | solution.py:50
  21.4 1.8 slice.133
  24.0 5.1 %collective-permute-start = (f32[8,65,128]{2,1,0:T(8,128)}, f32[8,65,128]{2,1,0:T(8,128)}, u32[]{:S(2)}, u32[]{:S(2)}) collective-permute-start(f32[8,65,128]{2,1,0:T(8,128)} %pad_maximum_fusion), channel_id=1, source_target_pairs={{8,0},{16,8},{24,16},{32,24},{40,32},{48,40},{56,48},{64,56},{72,6... | collective-permute-start | bytes 798728 | tf_op jit(solution)/shard_map/ppermute | solution.py:168
  29.2 2.4 copy.120
  32.9 1.3 reduce-window.16
  34.7 1.3 fusion.96
  36.1 2.3 fusion.20
  38.4 2.7 %slice.252 = bf16[4,8,64,128]{3,0,2,1:T(4,128)(2,1)} slice(f32[5,8,64,128]{3,0,2,1:T(8,128)} %convolution_bitcast_fusion), slice={[1:5], [0:8], [0:64], [0:128]} | slice | bytes 1048576 | tf_op jit(solution)/shard_map/slice | solution.py:52
  47.7 2.4 %copy.156 = bf16[16,8,16,256]{3,2,1,0:T(8,128)(2,1)} copy(bf16[16,8,16,256]{3,1,2,0:T(8,128)(2,1)} %bitcast.176) | data formatting | bytes 2097152
  52.6 2.7 %and_and_fusion = pred[16,256,256]{2,1,0:T(8,128)(4,1)S(1)} fusion(s32[16,256]{1,0:T(8,128)S(1)} %eq.84, pred[16,256]{1,0:T(8,128)(4,1)S(1)} %and.103, pred[256,256]{1,0:T(8,128)(4,1)} %iota_compare_fusion.1), kind=kLoop, calls=%fused_computation.15 | loop fusion | flops 3145728 | bytes 1134592 | tf_op jit(solution)/shard_map/and | solution.py:77
  56.8 1.5 fusion.33
  59.7 3.6 %fusion.18 = f32[4,256,8,64]{1,3,2,0:T(8,128)} fusion(f32[4,8,64,256]{3,2,1,0:T(8,128)S(1)} %fusion.33, f32[4,8,256]{2,1,0:T(8,128)S(1)} %copy-done.20, f32[4,256,256]{2,1,0:T(8,128)S(1)} %fusion.97, pred[256,256]{1,0:T(8,128)(4,1)S(1)} %copy-done.17, bf16[4,256,8,64]{1,0,3,2:T(4,128)(2,1)S(1)} %reshape.320, f32[4,256,8]{1,2,0:T(8,128)S(1)} %copy-done.18), kind=kOutput, calls=%fused_computation.26 | convolution fusion | flops 277872640 | bytes 6422528 | tf_op jit(solution)/shard_map/chst,cshp->cthp/dot_general | solution.py:84
  63.3 3.8 %fusion.3 = f32[16,2,256,64]{2,3,1,0:T(8,128)} fusion(f32[16,2,256]{2,1,0:T(2,128)S(1)} %bitcast.201, f32[16,256,256]{2,1,0:T(8,128)S(1)} %fusion.98, pred[16,256,256]{2,1,0:T(8,128)(4,1)S(1)} %and_and_fusion, bf16[16,256,2,64]{1,0,3,2:T(8,128)(2,1)S(1)} %bitcast.177), kind=kOutput, calls=%fused_computation.5 | convolution fusion | flops 276824064 | bytes 8421376 | tf_op jit(solution)/shard_map/chst,cshp->cthp/dot_general | solution.py:84
  69.4 1.5 collective-permute-start.1
  71.5 8.5 %collective-permute-done.1 = f32[8,65,128]{2,1,0:T(8,128)S(1)} collective-permute-done((f32[8,65,128]{2,1,0:T(8,128)S(1)}, f32[8,65,128]{2,1,0:T(8,128)S(1)}, u32[]{:S(2)}, u32[]{:S(2)}) %collective-permute-start.1) | collective-permute-done | bytes 266272 | tf_op jit(solution)/shard_map/ppermute | solution.py:168
  81.9 1.4 collective-permute-start.2
  83.3 2.0 fusion.19
  86.3 7.6 %collective-permute-done.2 = f32[8,65,128]{2,1,0:T(8,128)} collective-permute-done((f32[8,65,128]{2,1,0:T(8,128)}, f32[8,65,128]{2,1,0:T(8,128)}, u32[]{:S(2)}, u32[]{:S(2)}) %collective-permute-start.2) | collective-permute-done | bytes 266272 | tf_op jit(solution)/shard_map/ppermute | solution.py:168
  96.0 1.3 collective-permute-start.3
  97.3 2.5 %fusion.16 = bf16[16,256,2,64]{1,3,2,0:T(8,128)(2,1)} fusion(f32[16,2,256,64]{2,3,1,0:T(8,128)S(1)} %copy-done.6, bf16[16,256,128,1]{2,1,3,0:T(8,128)(2,1)S(1)} %bitcast.170, f32[16,256,2]{1,2,0:T(2,128)S(1)} %get-tuple-element.33, bf16[16,2,64,128]{3,0,2,1:T(8,128)(2,1)} %slice.153), kind=kOutput, calls=%fused_computation.21 | convolution fusion | flops 135790592 | bytes 4751360 | tf_op jit(solution)/shard_map/chpn,ctn->cthp/dot_general | solution.py:87
  99.8 5.5 %collective-permute-done.3 = f32[8,65,128]{2,1,0:T(8,128)S(1)} collective-permute-done((f32[8,65,128]{2,1,0:T(8,128)S(1)}, f32[8,65,128]{2,1,0:T(8,128)S(1)}, u32[]{:S(2)}, u32[]{:S(2)}) %collective-permute-start.3) | collective-permute-done | bytes 266272 | tf_op jit(solution)/shard_map/ppermute | solution.py:168
  106.4 1.3 collective-permute-start.4
  109.5 2.9 %copy.117 = f32[4,256,8,64]{1,0,3,2:T(4,128)S(1)} copy(f32[4,256,8,64]{1,3,2,0:T(8,128)} %fusion.18) | data formatting | bytes 4194304 | tf_op jit(solution)/shard_map/add | solution.py:98
  112.5 1.8 copy.152
  114.3 4.5 %copy.149 = bf16[16,256,2,64]{3,2,1,0:T(2,128)(2,1)S(1)} copy(bf16[16,256,2,64]{1,3,2,0:T(8,128)(2,1)} %fusion.16) | data formatting | bytes 2097152
  118.8 1.8 reshape.341
  120.6 1.1 multiply_reduce_fusion.1
  121.7 105.9 %all-reduce.5.cloned.1.call-done = f32[8,64,128]{2,1,0:T(8,128)} async-done(((f32[8,64,128]{2,1,0:T(8,128)}), f32[8,64,128]{2,1,0:T(8,128)}) %all-reduce.5.cloned.1.call-update) | async-done | bytes 262160 | tf_op jit(solution)/shard_map/psum | solution.py:156
  227.6 1.9 bitcast_multiply_fusion.1
  229.4 1.4 fusion.17
  230.9 2.3 copy.135
  (145 shorter events, 33.3 us)
Async XLA Ops:
  7.2 51.5 %copy-start = (bf16[4096,128]{1,0:T(8,128)(2,1)S(1)}, bf16[4096,128]{1,0:T(8,128)(2,1)}, u32[]{:S(2)}) copy-start(bf16[4096,128]{1,0:T(8,128)(2,1)} %param.14) | copy-start | bytes 3145732
  7.2 6.7 %copy-start.7 = (bf16[1024,512]{1,0:T(8,128)(2,1)S(1)}, bf16[1024,512]{1,0:T(8,128)(2,1)}, u32[]{:S(2)}) copy-start(bf16[1024,512]{1,0:T(8,128)(2,1)} %param.9) | copy-start | bytes 3145732
  7.2 100.6 %all-reduce.3.cloned.1.call-start = ((), (), s32[]{:S(2)}) async-start(), calls=%async_computation | async-start | bytes 131072 | tf_op jit(solution)/shard_map/psum | solution.py:137
  10.9 5.0 %copy-start.15 = (f32[1,8,8,128]{3,2,1,0:T(8,128)}, f32[1,8,8,128]{3,2,1,0:T(8,128)S(1)}, u32[]{:S(2)}) copy-start(f32[1,8,8,128]{3,2,1,0:T(8,128)S(1)} %fusion.109) | copy-start | bytes 98308
  14.4 2.7 %copy-start.8 = (bf16[1024,128]{1,0:T(8,128)(2,1)S(1)}, bf16[1024,128]{1,0:T(8,128)(2,1)}, u32[]{:S(2)}) copy-start(bf16[1024,128]{1,0:T(8,128)(2,1)} %param.11) | copy-start | bytes 786436
  17.5 11.6 %copy-start.13 = (s32[4096]{0:T(1024)S(1)}, s32[4096]{0:T(1024)}, u32[]{:S(2)}) copy-start(s32[4096]{0:T(1024)} %param.17) | copy-start | bytes 49156
  21.4 11.0 %copy-start.14 = (f32[2,4096]{1,0:T(2,128)S(1)}, f32[2,4096]{1,0:T(2,128)}, u32[]{:S(2)}) copy-start(f32[2,4096]{1,0:T(2,128)} %param.16) | copy-start | bytes 98308
  24.0 43.4 %collective-permute-start = (f32[8,65,128]{2,1,0:T(8,128)}, f32[8,65,128]{2,1,0:T(8,128)}, u32[]{:S(2)}, u32[]{:S(2)}) collective-permute-start(f32[8,65,128]{2,1,0:T(8,128)} %pad_maximum_fusion), channel_id=1, source_target_pairs={{8,0},{16,8},{24,16},{32,24},{40,32},{48,40},{56,48},{64,56},{72,6... | collective-permute-start | bytes 798728 | tf_op jit(solution)/shard_map/ppermute | solution.py:168
  29.2 6.9 %copy-start.2 = (bf16[4096,128]{1,0:T(8,128)(2,1)S(1)}, bf16[4096,128]{1,0:T(8,128)(2,1)}, u32[]{:S(2)}) copy-start(bf16[4096,128]{1,0:T(8,128)(2,1)} %param.15) | copy-start | bytes 3145732
  38.4 189.2 %all-reduce.5.cloned.1.call-start = ((), (), s32[]{:S(2)}) async-start(), calls=%async_computation.1 | async-start | bytes 524288 | tf_op jit(solution)/shard_map/psum | solution.py:156
  43.9 11.3 %copy-start.21 = (f32[15]{0:T(128)}, f32[15]{0:T(128)S(1)}, u32[]{:S(2)}) copy-start(f32[15]{0:T(128)S(1)} %convert_reduce_fusion) | copy-start | bytes 184
  52.6 5.8 %copy-start.4 = (bf16[1024,128]{1,0:T(8,128)(2,1)S(1)}, bf16[1024,128]{1,0:T(8,128)(2,1)}, u32[]{:S(2)}) copy-start(bf16[1024,128]{1,0:T(8,128)(2,1)} %param.10) | copy-start | bytes 786436
  52.6 5.8 %copy-start.9 = (bf16[1024,128]{1,0:T(8,128)(2,1)S(1)}, bf16[1024,128]{1,0:T(8,128)(2,1)}, u32[]{:S(2)}) copy-start(bf16[1024,128]{1,0:T(8,128)(2,1)} %param.11) | copy-start | bytes 786436
  58.7 1.0 copy-start.17
  58.7 1.0 copy-start.18
  58.7 1.0 copy-start.20
  59.7 3.7 %copy-start.3 = (bf16[16,8,16,256]{3,2,1,0:T(8,128)(2,1)S(1)}, bf16[16,8,16,256]{3,2,1,0:T(8,128)(2,1)}, u32[]{:S(2)}) copy-start(bf16[16,8,16,256]{3,2,1,0:T(8,128)(2,1)} %copy.156) | copy-start | bytes 3145732
  59.7 3.7 %copy-start.19 = (f32[2,16,256]{2,0,1:T(2,128)S(1)}, f32[2,16,256]{2,0,1:T(2,128)}, u32[]{:S(2)}) copy-start(f32[2,16,256]{2,0,1:T(2,128)} %copy.189) | copy-start | bytes 98308
  67.2 1.1 copy-start.22
  69.4 10.6 %collective-permute-start.1 = (f32[8,65,128]{2,1,0:T(8,128)S(1)}, f32[8,65,128]{2,1,0:T(8,128)S(1)}, u32[]{:S(2)}, u32[]{:S(2)}) collective-permute-start(f32[8,65,128]{2,1,0:T(8,128)S(1)} %pad_maximum_fusion.1), channel_id=1, source_target_pairs={{16,0},{24,8},{32,16},{40,24},{48,32},{56,40},{64,48},{72,56},{80,... | collective-permute-start | bytes 798728 | tf_op jit(solution)/shard_map/ppermute | solution.py:168
  80.0 5.2 %copy-start.11 = (f32[8,65,128]{2,1,0:T(8,128)}, f32[8,65,128]{2,1,0:T(8,128)S(1)}, u32[]{:S(2)}) copy-start(f32[8,65,128]{2,1,0:T(8,128)S(1)} %collective-permute-done.1) | copy-start | bytes 798724
  81.9 15.4 %copy-start.6 = (f32[16,2,256,64]{2,3,1,0:T(8,128)S(1)}, f32[16,2,256,64]{2,3,1,0:T(8,128)}, u32[]{:S(2)}) copy-start(f32[16,2,256,64]{2,3,1,0:T(8,128)} %fusion.3) | copy-start | bytes 6291460
  81.9 12.0 %collective-permute-start.2 = (f32[8,65,128]{2,1,0:T(8,128)}, f32[8,65,128]{2,1,0:T(8,128)}, u32[]{:S(2)}, u32[]{:S(2)}) collective-permute-start(f32[8,65,128]{2,1,0:T(8,128)} %pad_maximum_fusion.2), channel_id=1, source_target_pairs={{32,0},{40,8},{48,16},{56,24},{64,32},{72,40},{80,48},{88,56},{96,... | collective-permute-start | bytes 798728 | tf_op jit(solution)/shard_map/ppermute | solution.py:168
  96.0 9.3 %collective-permute-start.3 = (f32[8,65,128]{2,1,0:T(8,128)S(1)}, f32[8,65,128]{2,1,0:T(8,128)S(1)}, u32[]{:S(2)}, u32[]{:S(2)}) collective-permute-start(f32[8,65,128]{2,1,0:T(8,128)S(1)} %pad_maximum_fusion.3), channel_id=1, source_target_pairs={{64,0},{72,8},{80,16},{88,24},{96,32},{104,40},{112,48},{120,56},{... | collective-permute-start | bytes 798728 | tf_op jit(solution)/shard_map/ppermute | solution.py:168
  97.3 12.1 %copy-start.16 = (f32[1,8,8,128]{3,2,1,0:T(8,128)S(1)}, f32[1,8,8,128]{3,2,1,0:T(8,128)}, u32[]{:S(2)}) copy-start(f32[1,8,8,128]{3,2,1,0:T(8,128)} %copy-done.15) | copy-start | bytes 98308
  105.3 1.1 copy-start.12
  106.4 14.3 %collective-permute-start.4 = (f32[8,65,128]{2,1,0:T(8,128)}, f32[8,65,128]{2,1,0:T(8,128)}, u32[]{:S(2)}, u32[]{:S(2)}) collective-permute-start(f32[8,65,128]{2,1,0:T(8,128)} %pad_maximum_fusion.4), channel_id=1, source_target_pairs={{128,0},{136,8},{144,16},{152,24},{160,32},{168,40},{176,48},{184,... | collective-permute-start | bytes 798728 | tf_op jit(solution)/shard_map/ppermute | solution.py:168
  108.7 0.7 copy-start.10
  118.8 108.7 %copy-start.5 = (bf16[1024,128]{1,0:T(8,128)(2,1)S(1)}, bf16[1024,128]{1,0:T(8,128)(2,1)}, u32[]{:S(2)}) copy-start(bf16[1024,128]{1,0:T(8,128)(2,1)} %param.10) | copy-start | bytes 786436
  120.6 108.8 %copy-start.1 = (f32[64,8,4,256]{3,1,2,0:T(8,128)S(1)}, f32[64,8,4,256]{3,1,2,0:T(8,128)}, u32[]{:S(2)}) copy-start(f32[64,8,4,256]{3,1,2,0:T(8,128)} %copy.152) | copy-start | bytes 6291460
Sparse Core Ops, SparseCore 0:
  38.5 69.2 all-reduce.2
  111.0 116.4 all-reduce.4
where the time goes:
time: 241 us; the launch traced here: 240 us
  waiting for transfers between devices  128 us (53%)
  local copies, waits for them, and re-layouts  36.5 us (15%)
  other arithmetic  27.1 us (11%)
  matrix products  23.4 us (10%)
  between operations  14.6 us (6%)
  starting transfers between devices  10.6 us (4%)
    psum x1, waiting for transfers between devices, on_device(): my_heads = lax.psum(jnp.where(owned, slots, 0.0), 'seq')  106 us
    ppermute x5, waiting for transfers between devices, on_device(): got = lax.ppermute(message, 'seq', pairs)  21.7 us
    unnamed x57, local copies, waits for them, and re-layouts  17.3 us
    ppermute x5, starting transfers between devices, on_device(): got = lax.ppermute(message, 'seq', pairs)  10.6 us
    dot_general x2, matrix products, group_output(): jnp.einsum('chst,cshp->cthp', mixing, grad_group, preferred_element_type=...  7.47 us
    dot_general x2, matrix products, group_parts(): jnp.einsum('hcd,dhpn->chpn', coef, states, precision=lax.Precision.HIGHEST)  5.81 us
  transfers between devices with their start and end apart: 7, of which 5 were waited for; matrix products, arithmetic and copies ran while one was open for 27% of the time, Pallas kernels for 0%

commit v1 on v0

--- a/solution.py
+++ b/solution.py
@@ -153,7 +153,7 @@
         first_head % head_count,
         0,
     )
-    my_heads = lax.psum(jnp.where(owned, slots, 0.0), "seq")
+    my_heads = jnp.sum(lax.all_gather(jnp.where(owned, slots, 0.0), "seq"), axis=0)
     span_len = lax.axis_size("seq")
     whole_b = start_grad
     whole_a = jnp.exp(shard_total)

time: 241 us -> 212 us (0.88)
  the two profiles are of different devices: /device:TPU:1 before, /device:TPU:30 now
where the time goes in v1:
time: 212 us; the launch traced here: 211 us
  waiting for transfers between devices  92.5 us (44%)
  local copies, waits for them, and re-layouts  36.2 us (17%)
  other arithmetic  26.2 us (12%)
  starting transfers between devices  22.4 us (11%)
  matrix products  18.7 us (9%)
  between operations  14.7 us (7%)
    psum x1, waiting for transfers between devices, on_device(): summed_state = lax.psum(partial_state, 'resp')  75.1 us
    ppermute x5, starting transfers between devices, on_device(): got = lax.ppermute(message, 'seq', pairs)  22.3 us
    unnamed x81, local copies, waits for them, and re-layouts  18.7 us
    ppermute x5, waiting for transfers between devices, on_device(): got = lax.ppermute(message, 'seq', pairs)  17.3 us
    dot_general x2, matrix products, group_output(): jnp.einsum('chst,cshp->cthp', mixing, grad_group, preferred_element_type=...  7.54 us
    dot_general x2, matrix products, group_parts(): jnp.einsum('hcd,dhpn->chpn', coef, states, precision=lax.Precision.HIGHEST)  4.49 us
  transfers between devices with their start and end apart: 7, of which 4 were waited for; matrix products, arithmetic and copies ran while one was open for 29% of the time, Pallas kernels for 0%

profile of v1, /device:TPU:30, one launch (start us, length us, event | category | flops | bytes accessed | tf_op | source)
XLA Modules:
  0.0 210.7 jit_solution(11274825924101678788)
XLA Ops:
  12.4 1.5 copy.155
  14.4 1.1 fusion.20
  15.6 75.1 %all-reduce.2.cloned.1.call-done = f32[2,64,128]{2,1,0:T(8,128)} async-done(((f32[2,64,128]{2,1,0:T(8,128)}), f32[2,64,128]{2,1,0:T(8,128)}) %all-reduce.2.cloned.1.call-update) | async-done | bytes 65552 | tf_op jit(solution)/shard_map/psum | solution.py:137
  91.5 2.3 %reduce-window.14 = f32[8,8,128]{2,1,0:T(8,128)S(1)} reduce-window(f32[8,8,128]{2,1,0:T(8,128)S(1)} %copy.139, f32[]{:T(128)} %constant.29.clone.1), window={size=1x1x128 pad=0_0x0_0x127_0}, to_apply=%region_0.0 | reduce-window | flops 1040384 | bytes 65540 | tf_op jit(solution)/shard_map/reduce-window
  99.0 2.3 %copy.143 = bf16[1024,512]{0,1:T(8,128)(2,1)} copy(bf16[1024,512]{1,0:T(8,128)(2,1)} %param.9) | data formatting | bytes 2097152 | tf_op args[0]
  101.2 2.7 %reshape.322 = bf16[4,256,8,64]{1,0,3,2:T(4,128)(2,1)} reshape(bf16[1024,512]{0,1:T(8,128)(2,1)} %copy.143) | data formatting | bytes 2097152 | tf_op jit(solution)/shard_map/reshape | solution.py:24
  103.9 1.7 multiply_convert_fusion.5
  106.0 2.5 %convolution_bitcast_fusion = f32[5,8,64,128]{3,0,2,1:T(8,128)S(1)} fusion(f32[8,5,4,1]{1,2,3,0:T(4,128)S(1)} %copy.173, f32[4,8,64,128]{3,2,1,0:T(8,128)S(1)} %fusion.28), kind=kOutput, calls=%fused_computation.29 | convolution fusion | flops 15728640 | bytes 2359936 | tf_op jit(solution)/shard_map/hcd,dhpn->chpn/dot_general | solution.py:50
  108.6 1.4 copy-done.6
  111.5 1.9 collective-permute-start
  116.4 2.7 %slice.252 = bf16[4,8,64,128]{3,0,2,1:T(4,128)(2,1)} slice(f32[5,8,64,128]{3,0,2,1:T(8,128)} %copy-done.6), slice={[1:5], [0:8], [0:64], [0:128]} | slice | bytes 1048576 | tf_op jit(solution)/shard_map/slice | solution.py:52
  120.4 1.6 copy.162
  126.9 1.4 and_and_fusion
  129.6 3.7 %fusion.18 = f32[4,256,8,64]{1,3,2,0:T(8,128)} fusion(f32[4,8,64,256]{3,2,1,0:T(8,128)S(1)} %fusion.33, f32[4,8,256]{2,1,0:T(8,128)S(1)} %copy-done.26, f32[4,256,256]{2,1,0:T(8,128)S(1)} %fusion.97, pred[256,256]{1,0:T(8,128)(4,1)S(1)} %iota_compare_fusion.1, bf16[4,256,8,64]{1,0,3,2:T(4,128)(2,1)S(1)} %copy-done.5, f32[4,256,8]{1,2,0:T(8,128)S(1)} %copy-done.24), kind=kOutput, calls=%fused_computation.26 | convolution fusion | flops 277872640 | bytes 6422528 | tf_op jit(solution)/shard_map/chst,cshp->cthp/dot_general | solution.py:84
  133.3 3.9 %fusion.3 = f32[16,2,256,64]{2,3,1,0:T(8,128)} fusion(f32[16,2,256]{2,1,0:T(2,128)S(1)} %bitcast.203, f32[16,256,256]{2,1,0:T(8,128)S(1)} %fusion.98, pred[16,256,256]{2,1,0:T(8,128)(4,1)S(1)} %and_and_fusion, bf16[16,256,2,64]{1,0,3,2:T(8,128)(2,1)S(1)} %bitcast.179), kind=kOutput, calls=%fused_computation.5 | convolution fusion | flops 276824064 | bytes 8421376 | tf_op jit(solution)/shard_map/chst,cshp->cthp/dot_general | solution.py:84
  137.3 1.1 fusion.93
  139.6 2.7 %collective-permute-start.1 = (f32[8,65,128]{2,1,0:T(8,128)S(1)}, f32[8,65,128]{2,1,0:T(8,128)S(1)}, u32[]{:S(2)}, u32[]{:S(2)}) collective-permute-start(f32[8,65,128]{2,1,0:T(8,128)S(1)} %pad_maximum_fusion.1), channel_id=1, source_target_pairs={{16,0},{24,8},{32,16},{40,24},{48,32},{56,40},{64,48},{72,56},{80,... | collective-permute-start | bytes 798728 | tf_op jit(solution)/shard_map/ppermute | solution.py:168
  142.6 8.7 %collective-permute-done.1 = f32[8,65,128]{2,1,0:T(8,128)S(1)} collective-permute-done((f32[8,65,128]{2,1,0:T(8,128)S(1)}, f32[8,65,128]{2,1,0:T(8,128)S(1)}, u32[]{:S(2)}, u32[]{:S(2)}) %collective-permute-start.1) | collective-permute-done | bytes 266272 | tf_op jit(solution)/shard_map/ppermute | solution.py:168
  152.4 5.5 %collective-permute-start.2 = (f32[8,65,128]{2,1,0:T(8,128)S(1)}, f32[8,65,128]{2,1,0:T(8,128)S(1)}, u32[]{:S(2)}, u32[]{:S(2)}) collective-permute-start(f32[8,65,128]{2,1,0:T(8,128)S(1)} %pad_maximum_fusion.2), channel_id=1, source_target_pairs={{32,0},{40,8},{48,16},{56,24},{64,32},{72,40},{80,48},{88,56},{96,... | collective-permute-start | bytes 798728 | tf_op jit(solution)/shard_map/ppermute | solution.py:168
  158.5 5.6 %collective-permute-done.2 = f32[8,65,128]{2,1,0:T(8,128)S(1)} collective-permute-done((f32[8,65,128]{2,1,0:T(8,128)S(1)}, f32[8,65,128]{2,1,0:T(8,128)S(1)}, u32[]{:S(2)}, u32[]{:S(2)}) %collective-permute-start.2) | collective-permute-done | bytes 266272 | tf_op jit(solution)/shard_map/ppermute | solution.py:168
  165.2 5.7 %collective-permute-start.3 = (f32[8,65,128]{2,1,0:T(8,128)S(1)}, f32[8,65,128]{2,1,0:T(8,128)S(1)}, u32[]{:S(2)}, u32[]{:S(2)}) collective-permute-start(f32[8,65,128]{2,1,0:T(8,128)S(1)} %pad_maximum_fusion.3), channel_id=1, source_target_pairs={{64,0},{72,8},{80,16},{88,24},{96,32},{104,40},{112,48},{120,56},{... | collective-permute-start | bytes 798728 | tf_op jit(solution)/shard_map/ppermute | solution.py:168
  171.0 2.0 fusion.19
  173.2 3.0 %collective-permute-done.3 = f32[8,65,128]{2,1,0:T(8,128)S(1)} collective-permute-done((f32[8,65,128]{2,1,0:T(8,128)S(1)}, f32[8,65,128]{2,1,0:T(8,128)S(1)}, u32[]{:S(2)}, u32[]{:S(2)}) %collective-permute-start.3) | collective-permute-done | bytes 266272 | tf_op jit(solution)/shard_map/ppermute | solution.py:168
  177.3 6.4 %collective-permute-start.4 = (f32[8,65,128]{2,1,0:T(8,128)}, f32[8,65,128]{2,1,0:T(8,128)}, u32[]{:S(2)}, u32[]{:S(2)}) collective-permute-start(f32[8,65,128]{2,1,0:T(8,128)} %pad_maximum_fusion.4), channel_id=1, source_target_pairs={{128,0},{136,8},{144,16},{152,24},{160,32},{168,40},{176,48},{184,... | collective-permute-start | bytes 798728 | tf_op jit(solution)/shard_map/ppermute | solution.py:168
  183.7 1.5 fusion.16
  185.6 1.4 copy.152
  187.0 1.9 copy.187
  188.8 4.5 %copy.184 = bf16[16,256,2,64]{3,2,1,0:T(2,128)(2,1)S(1)} copy(bf16[16,256,2,64]{1,3,2,0:T(8,128)(2,1)} %fusion.16) | data formatting | bytes 2097152
  193.4 1.8 reshape.343
  196.2 4.0 %reduce_sum.29 = f32[8,64,128]{2,1,0:T(8,128)S(1)} reduce(f32[32,8,64,128]{3,2,1,0:T(8,128)} %all-gather.2.cloned.1.call-done, f32[]{:T(128)} %constant.29.clone.1), dimensions={0}, to_apply=%region_8.9 | reduce | flops 2031616 | bytes 8650756 | tf_op jit(solution)/shard_map/reduce_sum | solution.py:156
  200.3 1.7 bitcast_multiply_fusion.1
  202.5 1.3 copy.170
  (170 shorter events, 31.5 us)
Async XLA Ops:
  7.2 121.1 %copy-start = (bf16[4096,128]{1,0:T(8,128)(2,1)S(1)}, bf16[4096,128]{1,0:T(8,128)(2,1)}, u32[]{:S(2)}) copy-start(bf16[4096,128]{1,0:T(8,128)(2,1)} %param.14) | copy-start | bytes 3145732
  7.2 83.5 %all-reduce.2.cloned.1.call-start = ((), (), s32[]{:S(2)}) async-start(), calls=%async_computation | async-start | bytes 131072 | tf_op jit(solution)/shard_map/psum | solution.py:137
  10.6 3.8 %copy-start.2 = (bf16[4096,128]{1,0:T(8,128)(2,1)S(1)}, bf16[4096,128]{1,0:T(8,128)(2,1)}, u32[]{:S(2)}) copy-start(bf16[4096,128]{1,0:T(8,128)(2,1)} %param.15) | copy-start | bytes 3145732
  13.9 77.5 %copy-start.23 = (f32[8,1024]{1,0:T(8,128)S(1)}, f32[8,1024]{1,0:T(8,128)}, u32[]{:S(2)}) copy-start(f32[8,1024]{1,0:T(8,128)} %param.12) | copy-start | bytes 98308
  14.4 82.0 %copy-start.34 = (f32[4]{0:T(128)S(1)}, f32[4]{0:T(128)}, u32[]{:S(2)}) copy-start(f32[4]{0:T(128)} %constant.54.clone.1) | copy-start | bytes 52
  14.4 82.9 %copy-start.32 = (f32[5]{0:T(128)S(1)}, f32[5]{0:T(128)}, u32[]{:S(2)}) copy-start(f32[5]{0:T(128)} %constant.56.clone.1) | copy-start | bytes 64
  15.5 180.7 %all-gather.2.cloned.1.call-start = ((), (), s32[]{:S(2)}) async-start(), calls=%async_computation.1 | async-start | bytes 8650752 | tf_op jit(solution)/shard_map/all_gather | solution.py:156
  94.2 4.7 %copy-start.21 = (f32[1,8,8,128]{3,2,1,0:T(8,128)}, f32[1,8,8,128]{3,2,1,0:T(8,128)S(1)}, u32[]{:S(2)}) copy-start(f32[1,8,8,128]{3,2,1,0:T(8,128)S(1)} %fusion.109) | copy-start | bytes 98308
  94.4 15.8 %copy-start.28 = (f32[8,1]{0,1:T(1,128)}, f32[8,1]{0,1:T(1,128)S(1)}, u32[]{:S(2)}) copy-start(f32[8,1]{0,1:T(1,128)S(1)} %copy.186) | copy-start | bytes 100
  101.2 4.4 %copy-start.12 = (bf16[1024,128]{1,0:T(8,128)(2,1)S(1)}, bf16[1024,128]{1,0:T(8,128)(2,1)}, u32[]{:S(2)}) copy-start(bf16[1024,128]{1,0:T(8,128)(2,1)} %param.11) | copy-start | bytes 786436
  106.0 7.5 %copy-start.19 = (s32[4096]{0:T(1024)S(1)}, s32[4096]{0:T(1024)}, u32[]{:S(2)}) copy-start(s32[4096]{0:T(1024)} %param.17) | copy-start | bytes 49156
  110.0 9.2 %copy-start.20 = (f32[2,4096]{1,0:T(2,128)S(1)}, f32[2,4096]{1,0:T(2,128)}, u32[]{:S(2)}) copy-start(f32[2,4096]{1,0:T(2,128)} %param.16) | copy-start | bytes 98308
  111.5 25.8 %collective-permute-start = (f32[8,65,128]{2,1,0:T(8,128)}, f32[8,65,128]{2,1,0:T(8,128)}, u32[]{:S(2)}, u32[]{:S(2)}) collective-permute-start(f32[8,65,128]{2,1,0:T(8,128)} %pad_maximum_fusion), channel_id=1, source_target_pairs={{8,0},{16,8},{24,16},{32,24},{40,32},{48,40},{56,48},{64,56},{72,6... | collective-permute-start | bytes 798728 | tf_op jit(solution)/shard_map/ppermute | solution.py:168
  125.3 7.9 %copy-start.3 = (bf16[16,8,16,256]{3,2,1,0:T(8,128)(2,1)}, bf16[16,8,16,256]{3,2,1,0:T(8,128)(2,1)S(1)}, u32[]{:S(2)}) copy-start(bf16[16,8,16,256]{3,2,1,0:T(8,128)(2,1)S(1)} %copy.191) | copy-start | bytes 3145732
  129.6 3.7 %copy-start.25 = (f32[2,16,256]{2,0,1:T(2,128)S(1)}, f32[2,16,256]{2,0,1:T(2,128)}, u32[]{:S(2)}) copy-start(f32[2,16,256]{2,0,1:T(2,128)} %copy.224) | copy-start | bytes 98308
  133.3 3.9 %copy-start.31 = (f32[15]{0:T(128)S(1)}, f32[15]{0:T(128)}, u32[]{:S(2)}) copy-start(f32[15]{0:T(128)} %copy-done.30) | copy-start | bytes 184
  133.3 4.0 %copy-start.33 = (f32[8,1,1]{0,2,1:T(1,128)S(1)}, f32[8,1,1]{0,2,1:T(1,128)}, u32[]{:S(2)}) copy-start(f32[8,1,1]{0,2,1:T(1,128)} %get-tuple-element.43) | copy-start | bytes 100
  133.3 4.0 %copy-start.29 = (f32[8,1]{0,1:T(1,128)S(1)}, f32[8,1]{0,1:T(1,128)}, u32[]{:S(2)}) copy-start(f32[8,1]{0,1:T(1,128)} %copy-done.28) | copy-start | bytes 100
  137.1 5.2 %copy-start.4 = (bf16[16,8,16,256]{3,2,1,0:T(8,128)(2,1)S(1)}, bf16[16,8,16,256]{3,2,1,0:T(8,128)(2,1)}, u32[]{:S(2)}) copy-start(bf16[16,8,16,256]{3,2,1,0:T(8,128)(2,1)} %copy-done.3) | copy-start | bytes 3145732
  139.6 11.7 %collective-permute-start.1 = (f32[8,65,128]{2,1,0:T(8,128)S(1)}, f32[8,65,128]{2,1,0:T(8,128)S(1)}, u32[]{:S(2)}, u32[]{:S(2)}) collective-permute-start(f32[8,65,128]{2,1,0:T(8,128)S(1)} %pad_maximum_fusion.1), channel_id=1, source_target_pairs={{16,0},{24,8},{32,16},{40,24},{48,32},{56,40},{64,48},{72,56},{80,... | collective-permute-start | bytes 798728 | tf_op jit(solution)/shard_map/ppermute | solution.py:168
  152.4 11.7 %collective-permute-start.2 = (f32[8,65,128]{2,1,0:T(8,128)S(1)}, f32[8,65,128]{2,1,0:T(8,128)S(1)}, u32[]{:S(2)}, u32[]{:S(2)}) collective-permute-start(f32[8,65,128]{2,1,0:T(8,128)S(1)} %pad_maximum_fusion.2), channel_id=1, source_target_pairs={{32,0},{40,8},{48,16},{56,24},{64,32},{72,40},{80,48},{88,56},{96,... | collective-permute-start | bytes 798728 | tf_op jit(solution)/shard_map/ppermute | solution.py:168
  164.1 9.1 %copy-start.17 = (f32[8,65,128]{2,1,0:T(8,128)}, f32[8,65,128]{2,1,0:T(8,128)S(1)}, u32[]{:S(2)}) copy-start(f32[8,65,128]{2,1,0:T(8,128)S(1)} %collective-permute-done.2) | copy-start | bytes 798724
  165.2 18.5 %copy-start.9 = (f32[16,2,256,64]{2,3,1,0:T(8,128)S(1)}, f32[16,2,256,64]{2,3,1,0:T(8,128)}, u32[]{:S(2)}) copy-start(f32[16,2,256,64]{2,3,1,0:T(8,128)} %fusion.3) | copy-start | bytes 6291460
  165.2 11.0 %collective-permute-start.3 = (f32[8,65,128]{2,1,0:T(8,128)S(1)}, f32[8,65,128]{2,1,0:T(8,128)S(1)}, u32[]{:S(2)}, u32[]{:S(2)}) collective-permute-start(f32[8,65,128]{2,1,0:T(8,128)S(1)} %pad_maximum_fusion.3), channel_id=1, source_target_pairs={{64,0},{72,8},{80,16},{88,24},{96,32},{104,40},{112,48},{120,56},{... | collective-permute-start | bytes 798728 | tf_op jit(solution)/shard_map/ppermute | solution.py:168
  176.2 7.5 %copy-start.15 = (f32[8,65,128]{2,1,0:T(8,128)}, f32[8,65,128]{2,1,0:T(8,128)S(1)}, u32[]{:S(2)}) copy-start(f32[8,65,128]{2,1,0:T(8,128)S(1)} %collective-permute-done.3) | copy-start | bytes 798724
  177.3 18.0 %collective-permute-start.4 = (f32[8,65,128]{2,1,0:T(8,128)}, f32[8,65,128]{2,1,0:T(8,128)}, u32[]{:S(2)}, u32[]{:S(2)}) collective-permute-start(f32[8,65,128]{2,1,0:T(8,128)} %pad_maximum_fusion.4), channel_id=1, source_target_pairs={{128,0},{136,8},{144,16},{152,24},{160,32},{168,40},{176,48},{184,... | collective-permute-start | bytes 798728 | tf_op jit(solution)/shard_map/ppermute | solution.py:168
  183.7 1.9 copy-start.10
  193.4 1.8 copy-start.22
  196.2 4.1 %copy-start.8 = (bf16[1024,128]{1,0:T(8,128)(2,1)S(1)}, bf16[1024,128]{1,0:T(8,128)(2,1)}, u32[]{:S(2)}) copy-start(bf16[1024,128]{1,0:T(8,128)(2,1)} %param.10) | copy-start | bytes 786436
  196.2 4.1 %copy-start.16 = (f32[8,65,128]{2,1,0:T(8,128)S(1)}, f32[8,65,128]{2,1,0:T(8,128)}, u32[]{:S(2)}) copy-start(f32[8,65,128]{2,1,0:T(8,128)} %copy-done.15) | copy-start | bytes 798724
  196.2 4.1 %copy-start.18 = (f32[8,65,128]{2,1,0:T(8,128)S(1)}, f32[8,65,128]{2,1,0:T(8,128)}, u32[]{:S(2)}) copy-start(f32[8,65,128]{2,1,0:T(8,128)} %copy-done.17) | copy-start | bytes 798724
  200.3 1.8 copy-start.1
  (10 other events, 10.5 us)
Sparse Core Ops, SparseCore 0:
  15.6 74.9 all-reduce.1
  93.2 54.8 all-gather.1
